TPU v7x, 256 devices: a whole 4x4x8 slice. The times are simulated.
256 devices in a mesh: dp: 16 (over z_lo, y, core), tensor: 16 (over z_hi, x).
Axes of the slice: x: 4, y: 4, z: 8 (z_hi: 4, z_lo: 2; z = z_hi * 2 + z_lo), core: 2. Of those that a mesh axis runs over, the one named last changes fastest.
Arguments:
- attn_in: bfloat16 [4096, 4096], P('dp', 'tensor'), parts along dimension 0, may hold values from -127 to 127
- wo_int: bfloat16 [4096, 8192], P('tensor'), may hold values from -127 to 127
- wo_exponent: int32 [8192], replicated, may hold values from -15 to -12
- token_scale: float32 [4096], P(('dp', 'tensor')), parts along dimension 0, may hold values from 0.3 to 3
- residual: bfloat16 [4096, 8192], P(('dp', 'tensor')), parts along dimension 0, may hold values from -6 to 6
- norm_gain: float32 [8192], replicated, may hold values from 0.5 to 1.5
- gate_int: bfloat16 [8192, 4096], P(None, 'tensor'), may hold values from -127 to 127, as said below
- up_int: bfloat16 [8192, 4096], P(None, 'tensor'), may hold values from -127 to 127, as said below
- gate_exponent: int32 [4096], P('tensor'), may hold values from -14 to -12
- up_exponent: int32 [4096], P('tensor'), may hold values from -14 to -12
Outputs:
- hidden: bfloat16 [4096, 4096], P('dp', 'tensor'), parts along dimension 0
- checksum: float32 [256, 8192], P(('dp', 'tensor')), parts along dimension 0
There are 16 independent parts, one for each index of `dp`. A program takes and returns all parts, laid end to end along the dimension named above; an argument that names none is the same for every part. Nothing has to cross between parts.
Inputs may be any that keep to these rules, and one draw needn't show every extreme that they name: `gate_int`: integer values. `up_int`: integer values.
All inputs are finite; a program needn't handle non-finite values.
Results may differ from a plain program's by a relative error of at most 0.035.
Values may be sent and summed in bfloat16 or wider, within the bound.
No kernel may reach another device: no remote copies, remote signals or barrier semaphores. Data moves between devices by JAX's collectives and lax.ppermute only.
A program may use at most 64 MiB of HBM per device.

v0:
```python
import jax
import jax.numpy as jnp
from jax import lax
from jax.sharding import PartitionSpec as P


def normalize(stream, norm_gain):
    widened = stream.astype(jnp.float32)
    inverse = lax.rsqrt(jnp.mean(widened * widened, axis=1, keepdims=True) + 1e-05)
    return (widened * inverse * norm_gain[None, :]).astype(jnp.bfloat16)


def quantize(normed_low):
    widened = lax.optimization_barrier(normed_low).astype(jnp.float32)
    largest = jnp.max(jnp.abs(widened), axis=1, keepdims=True)
    xscale = ((largest + 1e-06) / 127.0).astype(jnp.bfloat16)
    levels = jnp.floor(widened / xscale.astype(jnp.float32) + 0.5).astype(jnp.bfloat16)
    return (levels, xscale)


def local(
    attn_in,
    wo_int,
    wo_exponent,
    token_scale,
    residual,
    norm_gain,
    gate_int,
    up_int,
    gate_exponent,
    up_exponent,
):
    groups = lax.axis_size("tensor")
    own_rows = residual.shape[0]
    col_scale = jnp.exp2(wo_exponent.astype(jnp.float32))
    gate_scale = jnp.exp2(gate_exponent.astype(jnp.float32))[None, :]
    up_scale = jnp.exp2(up_exponent.astype(jnp.float32))[None, :]
    partial_value = jnp.dot(attn_in, wo_int, preferred_element_type=jnp.float32)
    block_sums = jnp.sum(partial_value.reshape(groups, own_rows, partial_value.shape[1]), axis=1)
    owned_rows, col_total = (
        lax.psum_scatter(partial_value, "tensor", scatter_dimension=0, tiled=True),
        lax.psum_scatter(block_sums, "tensor", scatter_dimension=0, tiled=True),
    )
    checksum = col_total * col_scale[None, :] / own_rows
    attn_out = owned_rows * token_scale[:, None] * col_scale[None, :]
    stream = (residual.astype(jnp.float32) + attn_out).astype(jnp.bfloat16)
    normed_low = normalize(stream, norm_gain)
    all_normed = lax.all_gather(normed_low, "tensor", axis=0, tiled=True)
    levels, xscale = quantize(all_normed)
    row_scale = xscale.astype(jnp.float32)
    gate_sum = (
        jnp.dot(levels, gate_int, preferred_element_type=jnp.float32) * row_scale * gate_scale
    )
    up_sum = jnp.dot(levels, up_int, preferred_element_type=jnp.float32) * row_scale * up_scale
    hidden = (jax.nn.silu(gate_sum) * up_sum).astype(jnp.bfloat16)
    return (hidden, checksum)


def solution(mesh):
    placed = (
        P("dp", "tensor"),
        P("tensor", None),
        P(),
        P(("dp", "tensor")),
        P(("dp", "tensor"), None),
        P(),
        P(None, "tensor"),
        P(None, "tensor"),
        P("tensor"),
        P("tensor"),
    )
    return jax.shard_map(
        local,
        mesh=mesh,
        in_specs=placed,
        out_specs=(P("dp", "tensor"), P(("dp", "tensor"), None)),
        check_vma=False,
    )
```

profile of v0, /device:TPU:35, one launch (start us, length us, event | category | flops | bytes accessed | tf_op | source)
XLA Modules:
  0.0 402.2 jit_solution(13615173656178297063)
XLA Ops:
  7.2 0.0 copy-start
  7.2 0.0 reduce-scatter.2.cloned.1.call-start
  7.2 0.8 copy-done
  8.1 7.8 %bitcast_reduce_fusion = (f32[16,8192]{1,0:T(8,128)}, f32[256,8192]{1,0:T(8,128)}) fusion(bf16[256,256]{1,0:T(8,128)(2,1)S(1)} %copy-done, bf16[256,8192]{1,0:T(8,128)(2,1)} %param.11), kind=kOutput, calls=%fused_computation.6 | convolution fusion | flops 1075707904 | bytes 13238272 | tf_op jit(solution)/shard_map/dot_general | solution.py:38
  15.9 0.0 copy-start.4
  15.9 0.0 copy-start.2
  15.9 0.0 copy-start.7
  15.9 0.0 copy-start.3
  15.9 0.0 copy-start.9
  15.9 0.0 copy-start.5
  15.9 0.0 copy-start.6
  15.9 0.0 reduce-scatter.2.cloned.1.call-update
  15.9 0.0 all-reduce.3.cloned.1.call-start
  16.0 0.7 all-reduce.3.cloned.1.call-update
  16.7 0.0 all-gather.2.cloned.1.call-start
  16.7 0.0 copy-done.4
  16.8 121.8 %reduce-scatter.2.cloned.1.call-done = f32[16,8192]{1,0:T(8,128)} async-done(((f32[256,8192]{1,0:T(8,128)}), f32[16,8192]{1,0:T(8,128)}) %reduce-scatter.2.cloned.1.call-update) | async-done | bytes 524304 | tf_op jit(solution)/shard_map/reduce_scatter | solution.py:41
  138.6 0.0 copy-done.2
  138.6 0.0 copy-done.7
  138.6 1.3 fusion.8
  139.9 0.0 copy-done.3
  139.9 0.8 fusion.10
  140.8 0.0 all-gather.2.cloned.1.call-update
  140.8 0.0 copy-done.9
  140.8 0.6 dynamic-slice
  141.4 0.0 copy-done.5
  141.4 0.0 copy-done.6
  141.4 154.9 %all-reduce.3.cloned.1.call-done = f32[16,8192]{1,0:T(8,128)} async-done(((f32[16,8192]{1,0:T(8,128)}), f32[16,8192]{1,0:T(8,128)}) %all-reduce.3.cloned.1.call-update) | async-done | bytes 524304
  296.3 2.3 fusion.11
  298.5 87.6 %all-gather.2.cloned.1.call-done = bf16[256,8192]{1,0:T(8,128)(2,1)} async-done(((bf16[16,8192]{1,0:T(8,128)(2,1)}), bf16[256,8192]{1,0:T(8,128)(2,1)}) %all-gather.2.cloned.1.call-update) | async-done | bytes 4194320 | tf_op jit(solution)/shard_map/all_gather | solution.py:48
  386.1 0.0 copy-start.1
  386.1 3.2 fusion
  389.3 0.3 copy-done.1
  389.6 0.0 copy-start.8
  389.6 3.8 fusion.6
  393.3 0.0 copy-done.8
  393.4 2.3 fusion.7
  (5 shorter events, 0.0 us)
Async XLA Ops:
  7.2 0.9 copy-start
  7.2 131.4 %reduce-scatter.2.cloned.1.call-start = ((), (), s32[]{:S(2)}) async-start(), calls=%async_computation.1 | async-start | bytes 8912896 | tf_op jit(solution)/shard_map/reduce_scatter | solution.py:41
  15.9 0.9 copy-start.4
  15.9 122.7 %copy-start.2 = (bf16[16,8192]{1,0:T(8,128)(2,1)S(1)}, bf16[16,8192]{1,0:T(8,128)(2,1)}, u32[]{:S(2)}) copy-start(bf16[16,8192]{1,0:T(8,128)(2,1)} %param.14) | copy-start | bytes 786436
  15.9 122.7 %copy-start.7 = (f32[16]{0:T(128)S(1)}, f32[16]{0:T(128)}, u32[]{:S(2)}) copy-start(f32[16]{0:T(128)} %param.13) | copy-start | bytes 196
  15.9 124.0 %copy-start.3 = (f32[8192]{0:T(1024)S(1)}, f32[8192]{0:T(1024)}, u32[]{:S(2)}) copy-start(f32[8192]{0:T(1024)} %param.15) | copy-start | bytes 98308
  15.9 124.9 %copy-start.9 = (u32[256]{0:T(256)S(1)}, u32[256]{0:T(256)}, u32[]{:S(2)}) copy-start(u32[256]{0:T(256)} %constant.29) | copy-start | bytes 3076
  15.9 125.5 %copy-start.5 = (s32[256]{0:T(256)S(1)}, s32[256]{0:T(256)}, u32[]{:S(2)}) copy-start(s32[256]{0:T(256)} %param.18) | copy-start | bytes 3076
  15.9 125.5 %copy-start.6 = (s32[256]{0:T(256)S(1)}, s32[256]{0:T(256)}, u32[]{:S(2)}) copy-start(s32[256]{0:T(256)} %param.19) | copy-start | bytes 3076
  15.9 280.4 %all-reduce.3.cloned.1.call-start = ((), (), s32[]{:S(2)}) async-start(), calls=%async_computation.3 | async-start | bytes 1048576
  16.7 369.4 %all-gather.2.cloned.1.call-start = ((), (), s32[]{:S(2)}) async-start(), calls=%async_computation.2 | async-start | bytes 4456448 | tf_op jit(solution)/shard_map/all_gather | solution.py:48
  386.1 3.4 copy-start.1
  389.6 3.8 copy-start.8
Sparse Core Ops, SparseCore 0:
  16.0 122.4 reduce-scatter.1
  141.2 155.0 all-reduce.2
  298.7 87.3 all-gather.1
where the time goes:
time: 402 us
  waiting for transfers between devices  365 us (91%)
  matrix products  13.9 us (3%)
  between operations  13.8 us (3%)
  other arithmetic  7.64 us (2%)
    unnamed x4, waiting for transfers between devices  156 us
    reduce_scatter x1, waiting for transfers between devices, local(): lax.psum_scatter(partial_value, 'tensor', scatter_dimension=0, tiled=True)  122 us
    all_gather x1, waiting for transfers between devices, local(): all_normed = lax.all_gather(normed_low, 'tensor', axis=0, tiled=True)  87.6 us
  transfers between devices with their start and end apart: 3, of which 3 were waited for; matrix products, arithmetic and copies ran while one was open for 1% of the time, Pallas kernels for 0%

commit v1 on v0

--- a/solution.py
+++ b/solution.py
@@ -30,17 +30,13 @@
     gate_exponent,
     up_exponent,
 ):
-    groups = lax.axis_size("tensor")
     own_rows = residual.shape[0]
     col_scale = jnp.exp2(wo_exponent.astype(jnp.float32))
     gate_scale = jnp.exp2(gate_exponent.astype(jnp.float32))[None, :]
     up_scale = jnp.exp2(up_exponent.astype(jnp.float32))[None, :]
     partial_value = jnp.dot(attn_in, wo_int, preferred_element_type=jnp.float32)
-    block_sums = jnp.sum(partial_value.reshape(groups, own_rows, partial_value.shape[1]), axis=1)
-    owned_rows, col_total = (
-        lax.psum_scatter(partial_value, "tensor", scatter_dimension=0, tiled=True),
-        lax.psum_scatter(block_sums, "tensor", scatter_dimension=0, tiled=True),
-    )
+    owned_rows = lax.psum_scatter(partial_value, "tensor", scatter_dimension=0, tiled=True)
+    col_total = jnp.sum(owned_rows, axis=0, keepdims=True)
     checksum = col_total * col_scale[None, :] / own_rows
     attn_out = owned_rows * token_scale[:, None] * col_scale[None, :]
     stream = (residual.astype(jnp.float32) + attn_out).astype(jnp.bfloat16)

time: 402 us -> 233 us (0.58)
  waiting for transfers between devices: 365 us -> 198 us
    unnamed x4 -> x2, waiting for transfers between devices: 156 us -> 0.03 us
    all_gather x1, waiting for transfers between devices: 87.6 us -> 76.5 us  [local(): all_normed = lax.all_gather(normed_low, 'tensor', axis=0, tiled=True)]
  transfers between devices with their start and end apart: 3 -> 2, of which waited for: 3 -> 2; matrix products, arithmetic and copies ran while one was open for 1% -> 0% of each run, Pallas kernels for 0% -> 0%
where the time goes in v1:
time: 233 us
  waiting for transfers between devices  198 us (85%)
  between operations  14.1 us (6%)
  matrix products  12.8 us (5%)
  other arithmetic  6.08 us (3%)
    reduce_scatter x1, waiting for transfers between devices, local(): lax.psum_scatter(partial_value, 'tensor', scatter_dimension=0, tiled=True)  122 us
    all_gather x1, waiting for transfers between devices, local(): all_normed = lax.all_gather(normed_low, 'tensor', axis=0, tiled=True)  76.5 us
    dot_general x1, matrix products, local(): partial_value = jnp.dot(attn_in, wo_int, preferred_element_type=jnp.float32)  6.66 us
  transfers between devices with their start and end apart: 2, of which 2 were waited for; matrix products, arithmetic and copies ran while one was open for 0% of the time, Pallas kernels for 0%

profile of v1, /device:TPU:35, one launch (start us, length us, event | category | flops | bytes accessed | tf_op | source)
XLA Modules:
  0.0 232.9 jit_solution(13892100721113445172)
XLA Ops:
  7.2 0.0 copy-start
  7.2 0.0 reduce-scatter.2.cloned.1.call-start
  7.2 0.8 copy-done
  8.1 6.7 %fusion.14 = f32[256,8192]{1,0:T(8,128)} fusion(bf16[256,256]{1,0:T(8,128)(2,1)S(1)} %copy-done, bf16[256,8192]{1,0:T(8,128)(2,1)} %param.11), kind=kOutput, calls=%fused_computation.25 | convolution fusion | flops 1073741824 | bytes 12713984 | tf_op jit(solution)/shard_map/dot_general | solution.py:37
  14.7 0.0 copy-start.3
  14.7 0.0 copy-start.2
  14.7 0.0 copy-start.7
  14.7 0.0 copy-start.4
  14.7 0.0 copy-start.5
  14.8 0.0 copy-start.6
  14.8 0.0 reduce-scatter.2.cloned.1.call-update
  14.8 0.0 all-gather.2.cloned.1.call-start
  14.8 0.6 copy-done.3
  15.5 121.5 %reduce-scatter.2.cloned.1.call-done = f32[16,8192]{1,0:T(8,128)} async-done(((f32[256,8192]{1,0:T(8,128)}), f32[16,8192]{1,0:T(8,128)}) %reduce-scatter.2.cloned.1.call-update) | async-done | bytes 524304 | tf_op jit(solution)/shard_map/reduce_scatter | solution.py:38
  137.0 0.0 copy-done.2
  137.0 0.0 copy-done.7
  137.0 1.4 fusion.8
  138.4 0.0 copy-done.4
  138.4 0.8 fusion.10
  139.3 0.0 all-gather.2.cloned.1.call-update
  139.3 0.0 copy-done.5
  139.3 0.0 copy-done.6
  139.3 0.6 multiply_multiply_fusion
  140.0 76.5 %all-gather.2.cloned.1.call-done = bf16[256,8192]{1,0:T(8,128)(2,1)} async-done(((bf16[16,8192]{1,0:T(8,128)(2,1)}), bf16[256,8192]{1,0:T(8,128)(2,1)}) %all-gather.2.cloned.1.call-update) | async-done | bytes 4194320 | tf_op jit(solution)/shard_map/all_gather | solution.py:44
  216.5 0.0 copy-start.1
  216.5 3.2 %fusion = f32[256]{0:T(256)S(1)} fusion(bf16[256,8192]{1,0:T(8,128)(2,1)} %all-gather.2.cloned.1.call-done), kind=kLoop, calls=%fused_computation.2 | loop fusion | flops 6291200 | bytes 4195328 | tf_op jit(solution)/shard_map/reduce_max | solution.py:15
  219.7 0.3 copy-done.1
  220.0 0.0 copy-start.8
  220.0 3.8 %fusion.6 = f32[256,256]{1,0:T(8,128)S(1)} fusion(bf16[8192,256]{1,0:T(8,128)(2,1)} %param.16, f32[256]{0:T(256)S(1)} %multiply_exponential_fusion.2, f32[256]{0:T(256)S(1)} %fusion.11, bf16[256,8192]{1,0:T(8,128)(2,1)S(1)} %copy-done.1), kind=kOutput, calls=%fused_computation.10 | convolution fusion | flops 1084358656 | bytes 8652800 | tf_op jit(solution)/shard_map/dot_general | solution.py:48
  223.7 0.0 copy-done.8
  223.7 2.3 %fusion.7 = bf16[256,256]{1,0:T(8,128)(2,1)} fusion(bf16[8192,256]{1,0:T(8,128)(2,1)S(1)} %copy-done.8, f32[256,256]{1,0:T(8,128)S(1)} %fusion.6, f32[256]{0:T(256)S(1)} %multiply_exponential_fusion.1, f32[256]{0:T(256)S(1)} %fusion.11, bf16[256,8192]{1,0:T(8,128)(2,1)S(1)} %copy-done.1), kind=kOutput, calls=%fused_computation.11 | convolution fusion | flops 1084751872 | bytes 8783872 | tf_op jit(solution)/shard_map/dot_general | solution.py:50
  (5 shorter events, 0.0 us)
Async XLA Ops:
  7.2 0.9 copy-start
  7.2 129.8 %reduce-scatter.2.cloned.1.call-start = ((), (), s32[]{:S(2)}) async-start(), calls=%async_computation.1 | async-start | bytes 8912896 | tf_op jit(solution)/shard_map/reduce_scatter | solution.py:38
  14.7 0.8 copy-start.3
  14.7 122.3 %copy-start.2 = (bf16[16,8192]{1,0:T(8,128)(2,1)S(1)}, bf16[16,8192]{1,0:T(8,128)(2,1)}, u32[]{:S(2)}) copy-start(bf16[16,8192]{1,0:T(8,128)(2,1)} %param.14) | copy-start | bytes 786436
  14.7 122.3 %copy-start.7 = (f32[16]{0:T(128)S(1)}, f32[16]{0:T(128)}, u32[]{:S(2)}) copy-start(f32[16]{0:T(128)} %param.13) | copy-start | bytes 196
  14.7 123.7 %copy-start.4 = (f32[8192]{0:T(1024)S(1)}, f32[8192]{0:T(1024)}, u32[]{:S(2)}) copy-start(f32[8192]{0:T(1024)} %param.15) | copy-start | bytes 98308
  14.7 124.5 %copy-start.5 = (s32[256]{0:T(256)S(1)}, s32[256]{0:T(256)}, u32[]{:S(2)}) copy-start(s32[256]{0:T(256)} %param.18) | copy-start | bytes 3076
  14.8 124.6 %copy-start.6 = (s32[256]{0:T(256)S(1)}, s32[256]{0:T(256)}, u32[]{:S(2)}) copy-start(s32[256]{0:T(256)} %param.19) | copy-start | bytes 3076
  14.8 201.7 %all-gather.2.cloned.1.call-start = ((), (), s32[]{:S(2)}) async-start(), calls=%async_computation.2 | async-start | bytes 4456448 | tf_op jit(solution)/shard_map/all_gather | solution.py:44
  216.5 3.4 %copy-start.1 = (bf16[256,8192]{1,0:T(8,128)(2,1)S(1)}, bf16[256,8192]{1,0:T(8,128)(2,1)}, u32[]{:S(2)}) copy-start(bf16[256,8192]{1,0:T(8,128)(2,1)} %all-gather.2.cloned.1.call-done) | copy-start | bytes 12582916
  220.0 3.8 %copy-start.8 = (bf16[8192,256]{1,0:T(8,128)(2,1)S(1)}, bf16[8192,256]{1,0:T(8,128)(2,1)}, u32[]{:S(2)}) copy-start(bf16[8192,256]{1,0:T(8,128)(2,1)} %param.17) | copy-start | bytes 12582916
Sparse Core Ops, SparseCore 0:
  14.9 122.0 reduce-scatter.1
  139.4 77.0 all-gather.1
